TPU v7x, 512 devices: a whole 4x4x16 slice. The times are simulated.
512 devices in a mesh: grp: 16 (over x, y), clu: 32 (over z, core).
Axes of the slice: x: 4, y: 4, z: 16, core: 2. Of those that a mesh axis runs over, the one named last changes fastest.
Arguments:
- lower_inverse: bfloat16 [32, 2, 512, 512], P('clu', None, 'grp'), as said below
- upper_inverse: bfloat16 [32, 2, 512, 512], P('clu', None, 'grp'), as said below
- lower_factors: bfloat16 [32, 128, 2, 48, 512], P('clu', 'grp'), may hold values from -1.2578125 to 1.2578125
- upper_factors: bfloat16 [32, 128, 2, 48, 512], P('clu', 'grp'), may hold values from -1.2578125 to 1.2578125
- lower_ranks: int32 [32, 128], P('clu', 'grp'), may hold values from 16 to 48
- upper_ranks: int32 [32, 128], P('clu', 'grp'), may hold values from 16 to 48
- pivots: int32 [32, 512], P('clu'), may hold values from 0 to 511, each once within a row
- pair_lower: int32 [32, 512], P('clu', 'grp'), may hold values from 0 to 7
- pair_upper: int32 [32, 512], P('clu', 'grp'), may hold values from 0 to 7
- pair_owner: int32 [32, 512, 1], P('clu', 'grp'), may hold values from 0 to 31; in each aligned block of 32 rows (0 to 31, 32 to 63, ..., all dimensions but the last counted through in order) at most 2 rows name the same one
Outputs:
- lower_solved: bfloat16 [32, 128, 2, 48, 512], P('clu', 'grp')
- upper_solved: bfloat16 [32, 128, 2, 48, 512], P('clu', 'grp')
- arrived: bfloat16 [32, 16, 32, 2, 2, 2304], P('clu', 'grp')
Inputs may be any that keep to these rules, and one draw needn't show every extreme that they name: `lower_inverse`: each cluster's matrix is unit lower triangular: zeros above the diagonal, one on the real part's diagonal and zero on the imaginary part's. `upper_inverse`: each cluster's matrix is upper triangular: zeros below the diagonal in both parts. `pair_owner`: among the 32 pairs of one share, at most 2 name the same owner, and some share reaches it.
All inputs are finite; a program needn't handle non-finite values.
Results may differ from a plain program's by a relative error of at most 0.0058.
Values may be sent and summed in bfloat16 or wider, within the bound.
No kernel may reach another device: no remote copies, remote signals or barrier semaphores. Data moves between devices by JAX's collectives and lax.ppermute only.
A program may use at most 64 MiB of HBM per device.

v0:
```python
import jax
import jax.numpy as jnp
from jax import lax
from jax.sharding import PartitionSpec as P

SEND_CAP = 2


def mask_rows(factors, block_ranks):
    rank_width = factors.shape[2]
    row_index = lax.broadcasted_iota(jnp.int32, (factors.shape[0], rank_width), 1)
    row_mask = row_index < block_ranks[:, None]
    return jnp.where(row_mask[:, None, :, None], factors, jnp.zeros((), factors.dtype))


def product(left, right):
    return jnp.einsum("prb,psb->prs", left, right, preferred_element_type=jnp.float32)


def per_device(
    lower_inverse,
    upper_inverse,
    lower_factors,
    upper_factors,
    lower_ranks,
    upper_ranks,
    pivots,
    pair_lower,
    pair_upper,
    pair_owner,
):
    lower_masked = mask_rows(lower_factors[0], lower_ranks[0])
    upper_masked = mask_rows(upper_factors[0], upper_ranks[0])
    upper_pivoted = jnp.take(upper_masked, pivots[0], axis=3)
    block_count = lower_masked.shape[0]
    rank_width = lower_masked.shape[2]
    panel_count = lower_masked.shape[3]
    lower_real = lower_masked[:, 0].reshape(block_count * rank_width, panel_count)
    lower_imag = lower_masked[:, 1].reshape(block_count * rank_width, panel_count)
    upper_real = upper_pivoted[:, 0].reshape(block_count * rank_width, panel_count)
    upper_imag = upper_pivoted[:, 1].reshape(block_count * rank_width, panel_count)
    contract_last = (((1,), (1,)), ((), ()))
    lower_piece = lax.all_gather(lower_inverse, "grp", axis=2, tiled=True)
    upper_piece = lax.all_gather(upper_inverse, "grp", axis=2, tiled=True)
    piece_real = upper_piece[0, 0]
    piece_imag = upper_piece[0, 1]
    real_part = jnp.dot(lower_real, piece_real, preferred_element_type=jnp.float32) - jnp.dot(
        lower_imag, piece_imag, preferred_element_type=jnp.float32
    )
    imag_part = jnp.dot(lower_real, piece_imag, preferred_element_type=jnp.float32) + jnp.dot(
        lower_imag, piece_real, preferred_element_type=jnp.float32
    )
    lower_totals = jnp.stack([real_part, imag_part], 0)
    piece_real = lower_piece[0, 0]
    piece_imag = lower_piece[0, 1]
    real_part = lax.dot_general(
        upper_real, piece_real, contract_last, preferred_element_type=jnp.float32
    ) - lax.dot_general(upper_imag, piece_imag, contract_last, preferred_element_type=jnp.float32)
    imag_part = lax.dot_general(
        upper_real, piece_imag, contract_last, preferred_element_type=jnp.float32
    ) + lax.dot_general(upper_imag, piece_real, contract_last, preferred_element_type=jnp.float32)
    upper_totals = jnp.stack([real_part, imag_part], 0)
    lower_solved = jnp.transpose(
        lower_totals.astype(jnp.bfloat16).reshape(2, block_count, rank_width, panel_count),
        (1, 0, 2, 3),
    )
    upper_solved = jnp.transpose(
        upper_totals.astype(jnp.bfloat16).reshape(2, block_count, rank_width, panel_count),
        (1, 0, 2, 3),
    )
    left_blocks = lower_solved[pair_lower[0]]
    right_blocks = upper_solved[pair_upper[0]]
    pair_count = left_blocks.shape[0]
    real_part = product(left_blocks[:, 0], right_blocks[:, 0]) - product(
        left_blocks[:, 1], right_blocks[:, 1]
    )
    imag_part = product(left_blocks[:, 0], right_blocks[:, 1]) + product(
        left_blocks[:, 1], right_blocks[:, 0]
    )
    cores = (
        jnp.stack([real_part, imag_part], 1)
        .reshape(pair_count, 2 * rank_width * rank_width)
        .astype(jnp.bfloat16)
    )
    owners = pair_owner[0, :, 0]
    pair_ids = lax.broadcasted_iota(jnp.int32, (pair_count,), 0)
    same_owner = (owners[:, None] == owners[None, :]) & (pair_ids[None, :] < pair_ids[:, None])
    slots = jnp.sum(same_owner.astype(jnp.int32), axis=1)
    clusters = lax.axis_size("clu")
    target_slot = owners * SEND_CAP + slots
    slot_ids = lax.broadcasted_iota(jnp.int32, (clusters * SEND_CAP, pair_count), 0)
    one_hot = (slot_ids == target_slot[None, :]).astype(jnp.bfloat16)
    buffer = jnp.dot(one_hot, cores, preferred_element_type=jnp.float32).astype(jnp.bfloat16)
    buffer = buffer.reshape(clusters, SEND_CAP, 2, rank_width * rank_width)
    arrived = lax.all_to_all(buffer, "clu", split_axis=0, concat_axis=0, tiled=True)
    return (lower_solved[None], upper_solved[None], arrived[None, None])


def solution(mesh):
    in_specs = (
        P("clu", None, "grp", None),
        P("clu", None, "grp", None),
        P("clu", "grp", None, None, None),
        P("clu", "grp", None, None, None),
        P("clu", "grp"),
        P("clu", "grp"),
        P("clu", None),
        P("clu", "grp"),
        P("clu", "grp"),
        P("clu", "grp", None),
    )
    out_specs = (
        P("clu", "grp", None, None, None),
        P("clu", "grp", None, None, None),
        P("clu", "grp", None, None, None, None),
    )
    return jax.shard_map(
        per_device, mesh=mesh, in_specs=in_specs, out_specs=out_specs, check_vma=False
    )
```

profile of v0, /device:TPU:1, one launch (start us, length us, event | category | flops | bytes accessed | tf_op | source)
XLA Modules:
  0.0 210.7 jit_solution(4374763556248300210)
XLA Ops:
  7.2 0.7 all-gather.5.cloned.1.call-update
  8.0 0.7 all-gather.3.cloned.1.call-update
  8.7 2.6 %copy.48 = bf16[1,8,2,48,512]{3,1,4,2,0:T(8,128)(2,1)S(1)} copy(bf16[1,8,2,48,512]{4,3,2,1,0:T(8,128)(2,1)} %param.13) | data formatting | bytes 1572864 | tf_op args[3]
  11.4 2.5 %copy.43 = bf16[1,8,2,48,512]{3,1,4,2,0:T(8,128)(2,1)} copy(bf16[1,8,2,48,512]{4,3,2,1,0:T(8,128)(2,1)S(1)} %copy-done.8) | data formatting | bytes 1572864 | tf_op args[2]
  14.0 1.4 bitcast_select_fusion
  15.4 3.0 %gather_fusion = bf16[512,8,2,48]{3,1,2,0:T(8,128)(2,1)S(1)} fusion(bf16[8,2,48,512]{2,0,3,1:T(8,128)(2,1)} %bitcast_select_fusion, s32[1024]{0:T(1024)S(1)} %pad_clamp_fusion.2), kind=kCustom, calls=%fused_computation | custom fusion | bytes 1574912 | tf_op jit(solution)/shard_map/jit(_take)/gather | solution.py:34
  18.4 1.8 select_bitcast_fusion
  20.3 1.1 fusion.26
  21.4 2.6 %copy.49 = bf16[8,1,48,512]{3,2,0,1:T(8,128)(2,1)} copy(bf16[8,1,48,512]{2,0,1,3:T(8,128)(2,1)} %get-tuple-element.4) | data formatting | bytes 786432 | tf_op jit(solution)/shard_map/slice | solution.py:40
  24.0 0.7 copy.50
  24.8 1.1 fusion.27
  25.9 2.7 %copy.44 = bf16[8,1,48,512]{3,2,0,1:T(8,128)(2,1)} copy(bf16[8,1,48,512]{2,0,3,1:T(8,128)(2,1)} %get-tuple-element.6) | data formatting | bytes 786432 | tf_op jit(solution)/shard_map/slice | solution.py:38
  28.5 0.7 copy.45
  29.5 42.9 %all-gather.5.cloned.1.call-done = bf16[1,2,512,512]{3,2,1,0:T(8,128)(2,1)} async-done(((bf16[1,2,32,512]{3,2,1,0:T(8,128)(2,1)}), bf16[1,2,512,512]{3,2,1,0:T(8,128)(2,1)}) %all-gather.5.cloned.1.call-update) | async-done | bytes 1048592 | tf_op jit(solution)/shard_map/all_gather | solution.py:43
  72.4 2.3 %fusion.21 = f32[384,512]{1,0:T(8,128)} fusion(bf16[384,512]{1,0:T(8,128)(2,1)S(1)} %bitcast.132, bf16[1,2,512,512]{3,2,1,0:T(8,128)(2,1)} %all-gather.5.cloned.1.call-done), kind=kOutput, calls=%fused_computation.43 | convolution fusion | flops 201326592 | bytes 1703936 | tf_op jit(solution)/shard_map/dot_general | solution.py:59
  74.7 1.4 fusion.20
  76.2 56.5 %all-gather.3.cloned.1.call-done = bf16[1,2,512,512]{3,2,1,0:T(8,128)(2,1)} async-done(((bf16[1,2,32,512]{3,2,1,0:T(8,128)(2,1)}), bf16[1,2,512,512]{3,2,1,0:T(8,128)(2,1)}) %all-gather.3.cloned.1.call-update) | async-done | bytes 1048592 | tf_op jit(solution)/shard_map/all_gather | solution.py:44
  132.7 1.5 fusion.19
  134.2 1.4 fusion.18
  135.6 0.4 fusion.9
  136.0 0.4 fusion.8
  136.5 0.4 copy-done.2
  137.6 1.3 fusion.15
  138.9 2.4 %gather_fusion.1 = bf16[32,2,48,512]{3,2,1,0:T(8,128)(2,1)} fusion(bf16[8,2,48,512]{3,2,1,0:T(8,128)(2,1)S(1)} %get-tuple-element.12, s32[1024]{0:T(1024)S(1)} %pad_clamp_fusion.1), kind=kCustom, calls=%fused_computation.1 | custom fusion | bytes 6291584 | tf_op jit(solution)/shard_map/gather | solution.py:71
  141.3 2.4 %gather_fusion.2 = bf16[32,2,48,512]{3,2,1,0:T(8,128)(2,1)} fusion(bf16[8,2,48,512]{3,2,1,0:T(8,128)(2,1)S(1)} %get-tuple-element.7, s32[1024]{0:T(1024)S(1)} %pad_clamp_fusion), kind=kCustom, calls=%fused_computation.2 | custom fusion | bytes 6291584 | tf_op jit(solution)/shard_map/gather | solution.py:72
  143.8 2.6 %fusion = f32[32,48,48]{2,1,0:T(8,128)S(1)} fusion(bf16[32,2,48,512]{3,2,1,0:T(8,128)(2,1)} %gather_fusion.1, bf16[32,2,48,512]{3,2,1,0:T(8,128)(2,1)} %gather_fusion.2), kind=kOutput, calls=%fused_computation.11 | convolution fusion | flops 75497472 | bytes 3440640 | tf_op jit(solution)/shard_map/prb,psb->prs/dot_general | solution.py:17
  146.6 2.1 fusion.1
  149.0 0.6 fusion.13
  149.5 0.5 fusion.12
  150.3 1.4 convert_element_type.16
  152.2 50.9 %all_to_all.5 = bf16[32,2,2,2304]{3,2,1,0:T(2,128)(2,1)S(1)} all-to-all(bf16[32,2,2,2304]{3,2,1,0:T(2,128)(2,1)S(1)} %reshape.167), channel_id=1, replica_groups=mesh['grp'=16,'clu'=32] {'clu'}, dimensions={0} | all-to-all | bytes 1179648 | tf_op jit(solution)/shard_map/all_to_all | solution.py:95
  203.0 0.8 copy.63
  (49 shorter events, 2.6 us)
Async XLA Ops:
  7.2 4.1 %copy-start.10 = (s32[1,8]{1,0:T(1,128)S(1)}, s32[1,8]{1,0:T(1,128)}, u32[]{:S(2)}) copy-start(s32[1,8]{1,0:T(1,128)} %param.15) | copy-start | bytes 100
  7.2 4.2 %copy-start.9 = (s32[1,512]{1,0:T(1,128)S(1)}, s32[1,512]{1,0:T(1,128)}, u32[]{:S(2)}) copy-start(s32[1,512]{1,0:T(1,128)} %param.16) | copy-start | bytes 6148
  7.2 4.2 %copy-start.8 = (bf16[1,8,2,48,512]{4,3,2,1,0:T(8,128)(2,1)S(1)}, bf16[1,8,2,48,512]{4,3,2,1,0:T(8,128)(2,1)}, u32[]{:S(2)}) copy-start(bf16[1,8,2,48,512]{4,3,2,1,0:T(8,128)(2,1)} %param.12) | copy-start | bytes 2359300
  7.2 65.2 %all-gather.5.cloned.1.call-start = ((), (), s32[]{:S(2)}) async-start(), calls=%async_computation.2 | async-start | bytes 1114112 | tf_op jit(solution)/shard_map/all_gather | solution.py:43
  7.9 124.8 %all-gather.3.cloned.1.call-start = ((), (), s32[]{:S(2)}) async-start(), calls=%async_computation.1 | async-start | bytes 1114112 | tf_op jit(solution)/shard_map/all_gather | solution.py:44
  11.3 2.6 %copy-start.11 = (s32[1,8]{1,0:T(1,128)S(1)}, s32[1,8]{1,0:T(1,128)}, u32[]{:S(2)}) copy-start(s32[1,8]{1,0:T(1,128)} %param.14) | copy-start | bytes 100
  18.4 1.8 copy-start
  25.9 3.4 %copy-start.12 = (s32[1,32]{1,0:T(1,128)S(1)}, s32[1,32]{1,0:T(1,128)}, u32[]{:S(2)}) copy-start(s32[1,32]{1,0:T(1,128)} %param.17) | copy-start | bytes 388
  25.9 3.4 %copy-start.13 = (s32[1,32]{1,0:T(1,128)S(1)}, s32[1,32]{1,0:T(1,128)}, u32[]{:S(2)}) copy-start(s32[1,32]{1,0:T(1,128)} %param.18) | copy-start | bytes 388
  25.9 3.5 %copy-start.14 = (s32[1,32,1]{1,2,0:T(1,128)S(1)}, s32[1,32,1]{1,2,0:T(1,128)}, u32[]{:S(2)}) copy-start(s32[1,32,1]{1,2,0:T(1,128)} %param.19) | copy-start | bytes 388
  25.9 46.5 %copy-start.3 = (bf16[8,1,48,512]{3,2,0,1:T(8,128)(2,1)S(1)}, bf16[8,1,48,512]{3,2,0,1:T(8,128)(2,1)}, u32[]{:S(2)}) copy-start(bf16[8,1,48,512]{3,2,0,1:T(8,128)(2,1)} %copy.49) | copy-start | bytes 1179652
  29.3 103.4 %copy-start.4 = (bf16[8,1,48,512]{3,2,0,1:T(8,128)(2,1)S(1)}, bf16[8,1,48,512]{3,2,0,1:T(8,128)(2,1)}, u32[]{:S(2)}) copy-start(bf16[8,1,48,512]{3,2,0,1:T(8,128)(2,1)} %copy.44) | copy-start | bytes 1179652
  76.2 59.4 %copy-start.1 = (bf16[1,2,512,512]{3,2,1,0:T(8,128)(2,1)S(1)}, bf16[1,2,512,512]{3,2,1,0:T(8,128)(2,1)}, u32[]{:S(2)}) copy-start(bf16[1,2,512,512]{3,2,1,0:T(8,128)(2,1)} %all-gather.5.cloned.1.call-done) | copy-start | bytes 3145732
  132.7 2.9 %copy-start.7 = (f32[384,512]{1,0:T(8,128)S(1)}, f32[384,512]{1,0:T(8,128)}, u32[]{:S(2)}) copy-start(f32[384,512]{1,0:T(8,128)} %fusion.21) | copy-start | bytes 2359300
  135.6 1.2 copy-start.2
  143.8 2.8 %copy-start.5 = (bf16[32,2,48,512]{3,2,1,0:T(8,128)(2,1)S(1)}, bf16[32,2,48,512]{3,2,1,0:T(8,128)(2,1)}, u32[]{:S(2)}) copy-start(bf16[32,2,48,512]{3,2,1,0:T(8,128)(2,1)} %gather_fusion.1) | copy-start | bytes 9437188
  146.6 2.4 %copy-start.6 = (bf16[32,2,48,512]{3,2,1,0:T(8,128)(2,1)S(1)}, bf16[32,2,48,512]{3,2,1,0:T(8,128)(2,1)}, u32[]{:S(2)}) copy-start(bf16[32,2,48,512]{3,2,1,0:T(8,128)(2,1)} %gather_fusion.2) | copy-start | bytes 9437188
Sparse Core Ops, SparseCore 0:
  11.1 61.2 all-gather.4
  75.5 57.1 all-gather.2
where the time goes:
time: 211 us
  waiting for transfers between devices  101 us (48%)
  blocking collectives  50.9 us (24%)
  local copies, waits for them, and re-layouts  25.2 us (12%)
  between operations  14.4 us (7%)
  matrix products  14.2 us (7%)
  other arithmetic  5.23 us (2%)
    all_gather x1, waiting for transfers between devices, per_device(): upper_piece = lax.all_gather(upper_inverse, 'grp', axis=2, tiled=True)  56.5 us
    all_to_all x1, blocking collectives, per_device(): lax.all_to_all(buffer, 'clu', split_axis=0, concat_axis=0, tiled=True)  50.9 us
    all_gather x1, waiting for transfers between devices, per_device(): lower_piece = lax.all_gather(lower_inverse, 'grp', axis=2, tiled=True)  42.9 us
    unnamed x33, local copies, waits for them, and re-layouts  6.88 us
    dot_general x4, matrix products, product(): jnp.einsum('prb,psb->prs', left, right, preferred_element_type=jnp.float32)  5.78 us
  transfers between devices with their start and end apart: 2, of which 2 were waited for; matrix products, arithmetic and copies ran while one was open for 12% of the time, Pallas kernels for 0%

commit v1 on v0

--- a/solution.py
+++ b/solution.py
@@ -1,9 +1,47 @@
+import functools
 import jax
 import jax.numpy as jnp
 from jax import lax
 from jax.sharding import PartitionSpec as P
 
 SEND_CAP = 2
+
+
+def form_ticks(state, at_axis):
+    state = jnp.moveaxis(state, 0, at_axis)
+    row_out = state.shape
+    return state.reshape(
+        *row_out[:at_axis], row_out[at_axis] * row_out[at_axis + 1], *row_out[at_axis + 2 :]
+    )
+
+
+def turn_group_on(u_in, chip_axis, dim_no):
+    n = lax.axis_size(chip_axis)
+    seen_now = range(n)
+    u_next = map(lambda hop_no: (hop_no, (hop_no + 1) % n), seen_now)
+    kept_rows = list(u_next)
+    val2, frame_out = ([], [])
+    panels = [(j, src_i) for src_i, j in kept_rows]
+    for dev in range(n - 1):
+        if dev % 2 == 0:
+            found_now = lax.ppermute(
+                val2[-1] if val2 else u_in, axis_name=chip_axis, perm=kept_rows
+            )
+            val2.append(found_now)
+        else:
+            tall = lax.ppermute(
+                frame_out[-1] if frame_out else u_in, axis_name=chip_axis, perm=panels
+            )
+            frame_out.append(tall)
+    val = jnp.stack([*val2[::-1], u_in, *frame_out], 0)
+    local_now = len(val2)
+    base_arr = lax.axis_index(chip_axis)
+    t1 = base_arr - local_now
+    val = val[(jnp.arange(n) - t1) % n]
+    return form_ticks(val, dim_no)
+
+
+fix_cards = functools.partial(turn_group_on, chip_axis="grp", dim_no=2)
 
 
 def mask_rows(factors, block_ranks):
@@ -41,7 +79,7 @@
     upper_imag = upper_pivoted[:, 1].reshape(block_count * rank_width, panel_count)
     contract_last = (((1,), (1,)), ((), ()))
     lower_piece = lax.all_gather(lower_inverse, "grp", axis=2, tiled=True)
-    upper_piece = lax.all_gather(upper_inverse, "grp", axis=2, tiled=True)
+    upper_piece = fix_cards(upper_inverse)
     piece_real = upper_piece[0, 0]
     piece_imag = upper_piece[0, 1]
     real_part = jnp.dot(lower_real, piece_real, preferred_element_type=jnp.float32) - jnp.dot(

time: 211 us -> 199 us (0.943)
  waiting for transfers between devices: 101 us -> 6.34 us
  starting transfers between devices: 0.08 us -> 63.3 us
  local copies, waits for them, and re-layouts: 25.2 us -> 37.8 us
  blocking collectives: 50.9 us -> 58.4 us
  matrix products: 14.2 us -> 11.3 us
    ppermute x0 -> x15, starting transfers between devices: none -> 63.3 us  [the longest x7 45.8 us: turn_group_on(): lax.ppermute(frame_out[-1] if frame_out else u_in, axis_name=chip_axis, p...]
    all_gather x1 -> x0, waiting for transfers between devices: 56.5 us -> none  [per_device(): upper_piece = lax.all_gather(upper_inverse, 'grp', axis=2, tiled=True)]
    all_gather x1, waiting for transfers between devices: 42.9 us -> 0.02 us  [per_device(): lower_piece = lax.all_gather(lower_inverse, 'grp', axis=2, tiled=True)]
    unnamed x33 -> x62, local copies, waits for them, and re-layouts: 6.88 us -> 20 us
    all_to_all x1, blocking collectives: 50.9 us -> 58.4 us  [per_device(): lax.all_to_all(buffer, 'clu', split_axis=0, concat_axis=0, tiled=True)]
    ppermute x0 -> x15, waiting for transfers between devices: none -> 6.3 us  [the longest x8 6.28 us: turn_group_on(): lax.ppermute(val2[-1] if val2 else u_in, axis_name=chip_axis, perm=kept_r...]
  transfers between devices with their start and end apart: 2 -> 16, of which waited for: 2 -> 2; matrix products, arithmetic and copies ran while one was open for 12% -> 18% of each run, Pallas kernels for 0% -> 0%
where the time goes in v1:
time: 199 us; the launch traced here: 198 us
  starting transfers between devices  63.3 us (32%)
  blocking collectives  58.4 us (29%)
  local copies, waits for them, and re-layouts  37.8 us (19%)
  between operations  14.7 us (7%)
  matrix products  11.3 us (6%)
  waiting for transfers between devices  6.34 us (3%)
  other arithmetic  5.89 us (3%)
    all_to_all x1, blocking collectives, per_device(): lax.all_to_all(buffer, 'clu', split_axis=0, concat_axis=0, tiled=True)  58.4 us
    ppermute x7, starting transfers between devices, turn_group_on(): lax.ppermute(frame_out[-1] if frame_out else u_in, axis_name=chip_axis, p...  45.8 us
    unnamed x62, local copies, waits for them, and re-layouts  20 us
    ppermute x8, starting transfers between devices, turn_group_on(): lax.ppermute(val2[-1] if val2 else u_in, axis_name=chip_axis, perm=kept_r...  17.4 us
    ppermute x8, waiting for transfers between devices, turn_group_on(): lax.ppermute(val2[-1] if val2 else u_in, axis_name=chip_axis, perm=kept_r...  6.28 us
    dot_general x4, matrix products, product(): jnp.einsum('prb,psb->prs', left, right, preferred_element_type=jnp.float32)  5.77 us
  transfers between devices with their start and end apart: 16, of which 2 were waited for; matrix products, arithmetic and copies ran while one was open for 18% of the time, Pallas kernels for 0%

profile of v1, /device:TPU:1, one launch (start us, length us, event | category | flops | bytes accessed | tf_op | source)
XLA Modules:
  0.0 197.7 jit_solution(2051371274657716711)
XLA Ops:
  7.2 4.0 %collective-permute-start = (bf16[1,2,32,512]{3,2,1,0:T(8,128)(2,1)}, bf16[1,2,32,512]{3,2,1,0:T(8,128)(2,1)S(1)}, u32[]{:S(2)}, u32[]{:S(2)}) collective-permute-start(bf16[1,2,32,512]{3,2,1,0:T(8,128)(2,1)} %param.11), channel_id=1, source_target_pairs={{0,32},{32,64},{64,96},{96,128},{128,160},{160,192},{192,224},{224... | collective-permute-start | bytes 196616 | tf_op jit(solution)/shard_map/ppermute | solution.py:27
  11.3 5.6 %collective-permute-start.8 = (bf16[1,2,32,512]{3,2,1,0:T(8,128)(2,1)}, bf16[1,2,32,512]{3,2,1,0:T(8,128)(2,1)S(1)}, u32[]{:S(2)}, u32[]{:S(2)}) collective-permute-start(bf16[1,2,32,512]{3,2,1,0:T(8,128)(2,1)} %param.11), channel_id=1, source_target_pairs={{32,0},{64,32},{96,64},{128,96},{160,128},{192,160},{224,192},{256... | collective-permute-start | bytes 196616 | tf_op jit(solution)/shard_map/ppermute | solution.py:32
  16.9 2.6 %copy.76 = bf16[1,8,2,48,512]{3,1,4,2,0:T(8,128)(2,1)S(1)} copy(bf16[1,8,2,48,512]{4,3,2,1,0:T(8,128)(2,1)} %param.13) | data formatting | bytes 1572864 | tf_op args[3]
  19.6 1.5 bitcast_select_fusion
  21.1 3.0 %gather_fusion.1 = bf16[512,8,2,48]{3,1,2,0:T(8,128)(2,1)S(1)} fusion(bf16[8,2,48,512]{2,0,3,1:T(8,128)(2,1)} %bitcast_select_fusion, s32[1024]{0:T(1024)S(1)} %pad_clamp_fusion.2), kind=kCustom, calls=%fused_computation.1 | custom fusion | bytes 1574912 | tf_op jit(solution)/shard_map/jit(_take)/gather | solution.py:72
  24.0 1.8 select_bitcast_fusion
  26.9 2.6 %copy.57 = bf16[1,8,2,48,512]{3,1,4,2,0:T(8,128)(2,1)S(1)} copy(bf16[1,8,2,48,512]{4,3,2,1,0:T(8,128)(2,1)} %param.12) | data formatting | bytes 1572864 | tf_op args[2]
  30.9 1.9 collective-permute-start.1
  33.0 6.2 %collective-permute-done.1 = bf16[1,2,32,512]{3,2,1,0:T(8,128)(2,1)S(1)} collective-permute-done((bf16[1,2,32,512]{3,2,1,0:T(8,128)(2,1)S(1)}, bf16[1,2,32,512]{3,2,1,0:T(8,128)(2,1)S(1)}, u32[]{:S(2)}, u32[]{:S(2)}) %collective-permute-start.1) | collective-permute-done | bytes 65568 | tf_op jit(solution)/shard_map/ppermute | solution.py:27
  39.2 1.9 collective-permute-start.2
  41.2 6.7 %collective-permute-start.9 = (bf16[1,2,32,512]{3,2,1,0:T(8,128)(2,1)S(1)}, bf16[1,2,32,512]{3,2,1,0:T(8,128)(2,1)}, u32[]{:S(2)}, u32[]{:S(2)}) collective-permute-start(bf16[1,2,32,512]{3,2,1,0:T(8,128)(2,1)S(1)} %collective-permute-done.8), channel_id=1, source_target_pairs={{32,0},{64,32},{96,64},{128,96},{160,128},{192,160},{224,192},{256... | collective-permute-start | bytes 196616 | tf_op jit(solution)/shard_map/ppermute | solution.py:32
  47.9 1.9 collective-permute-start.3
  49.9 6.7 %collective-permute-start.10 = (bf16[1,2,32,512]{3,2,1,0:T(8,128)(2,1)}, bf16[1,2,32,512]{3,2,1,0:T(8,128)(2,1)}, u32[]{:S(2)}, u32[]{:S(2)}) collective-permute-start(bf16[1,2,32,512]{3,2,1,0:T(8,128)(2,1)} %collective-permute-done.9), channel_id=1, source_target_pairs={{32,0},{64,32},{96,64},{128,96},{160,128},{192,160},{224,192},{256... | collective-permute-start | bytes 196616 | tf_op jit(solution)/shard_map/ppermute | solution.py:32
  56.6 1.9 collective-permute-start.4
  59.1 1.5 copy.77
  63.3 6.7 %collective-permute-start.11 = (bf16[1,2,32,512]{3,2,1,0:T(8,128)(2,1)}, bf16[1,2,32,512]{3,2,1,0:T(8,128)(2,1)S(1)}, u32[]{:S(2)}, u32[]{:S(2)}) collective-permute-start(bf16[1,2,32,512]{3,2,1,0:T(8,128)(2,1)} %collective-permute-done.10), channel_id=1, source_target_pairs={{32,0},{64,32},{96,64},{128,96},{160,128},{192,160},{224,192},{256... | collective-permute-start | bytes 196616 | tf_op jit(solution)/shard_map/ppermute | solution.py:32
  70.0 1.9 collective-permute-start.5
  72.0 6.7 %collective-permute-start.12 = (bf16[1,2,32,512]{3,2,1,0:T(8,128)(2,1)S(1)}, bf16[1,2,32,512]{3,2,1,0:T(8,128)(2,1)S(1)}, u32[]{:S(2)}, u32[]{:S(2)}) collective-permute-start(bf16[1,2,32,512]{3,2,1,0:T(8,128)(2,1)S(1)} %collective-permute-done.11), channel_id=1, source_target_pairs={{32,0},{64,32},{96,64},{128,96},{160,128},{192,160},{224,192},{256... | collective-permute-start | bytes 196616 | tf_op jit(solution)/shard_map/ppermute | solution.py:32
  78.7 1.9 collective-permute-start.6
  80.6 6.7 %collective-permute-start.13 = (bf16[1,2,32,512]{3,2,1,0:T(8,128)(2,1)S(1)}, bf16[1,2,32,512]{3,2,1,0:T(8,128)(2,1)S(1)}, u32[]{:S(2)}, u32[]{:S(2)}) collective-permute-start(bf16[1,2,32,512]{3,2,1,0:T(8,128)(2,1)S(1)} %collective-permute-done.12), channel_id=1, source_target_pairs={{32,0},{64,32},{96,64},{128,96},{160,128},{192,160},{224,192},{256... | collective-permute-start | bytes 196616 | tf_op jit(solution)/shard_map/ppermute | solution.py:32
  87.3 1.9 collective-permute-start.7
  89.3 6.9 %collective-permute-start.14 = (bf16[1,2,32,512]{3,2,1,0:T(8,128)(2,1)S(1)}, bf16[1,2,32,512]{3,2,1,0:T(8,128)(2,1)S(1)}, u32[]{:S(2)}, u32[]{:S(2)}) collective-permute-start(bf16[1,2,32,512]{3,2,1,0:T(8,128)(2,1)S(1)} %collective-permute-done.13), channel_id=1, source_target_pairs={{32,0},{64,32},{96,64},{128,96},{160,128},{192,160},{224,192},{256... | collective-permute-start | bytes 196616 | tf_op jit(solution)/shard_map/ppermute | solution.py:32
  98.0 1.5 bitcast_dynamic-update-slice_fusion.9
  99.5 1.5 bitcast_dynamic-update-slice_fusion.8
  105.6 1.5 bitcast_dynamic-update-slice_fusion.3
  109.5 1.8 gather_fusion
  113.2 1.5 fusion.21
  118.4 2.4 %gather_fusion.2 = bf16[32,2,48,512]{3,2,1,0:T(8,128)(2,1)} fusion(bf16[8,2,48,512]{3,2,1,0:T(8,128)(2,1)S(1)} %get-tuple-element.14, s32[1024]{0:T(1024)S(1)} %get-tuple-element.12), kind=kCustom, calls=%fused_computation.2 | custom fusion | bytes 6291584 | tf_op jit(solution)/shard_map/gather | solution.py:109
  120.8 2.4 %gather_fusion.3 = bf16[32,2,48,512]{3,2,1,0:T(8,128)(2,1)} fusion(bf16[8,2,48,512]{3,2,1,0:T(8,128)(2,1)S(1)} %get-tuple-element.7, s32[1024]{0:T(1024)S(1)} %get-tuple-element.11), kind=kCustom, calls=%fused_computation.3 | custom fusion | bytes 6291584 | tf_op jit(solution)/shard_map/gather | solution.py:110
  123.2 2.6 %fusion = f32[32,48,48]{2,1,0:T(8,128)S(1)} fusion(bf16[32,2,48,512]{3,2,1,0:T(8,128)(2,1)} %gather_fusion.2, bf16[32,2,48,512]{3,2,1,0:T(8,128)(2,1)} %gather_fusion.3), kind=kOutput, calls=%fused_computation.12 | convolution fusion | flops 75497472 | bytes 3440640 | tf_op jit(solution)/shard_map/prb,psb->prs/dot_general | solution.py:55
  126.0 2.1 %fusion.1 = f32[32,48,48]{2,1,0:T(8,128)S(1)} fusion(bf16[32,2,48,512]{3,2,1,0:T(8,128)(2,1)S(1)} %copy-done.4, bf16[32,2,48,512]{3,2,1,0:T(8,128)(2,1)} %gather_fusion.3), kind=kOutput, calls=%fused_computation.13 | convolution fusion | flops 75497472 | bytes 3440640 | tf_op jit(solution)/shard_map/prb,psb->prs/dot_general | solution.py:55
  131.6 58.4 %all_to_all.5 = bf16[32,2,2,2304]{3,2,1,0:T(2,128)(2,1)S(1)} all-to-all(bf16[32,2,2,2304]{3,2,1,0:T(2,128)(2,1)S(1)} %reshape.220), channel_id=1, replica_groups=mesh['grp'=16,'clu'=32] {'clu'}, dimensions={0} | all-to-all | bytes 1179648 | tf_op jit(solution)/shard_map/all_to_all | solution.py:133
  (109 shorter events, 25.0 us)
Async XLA Ops:
  7.2 12.3 %copy-start.17 = (s32[1,8]{1,0:T(1,128)S(1)}, s32[1,8]{1,0:T(1,128)}, u32[]{:S(2)}) copy-start(s32[1,8]{1,0:T(1,128)} %param.15) | copy-start | bytes 100
  7.2 12.4 %copy-start.15 = (s32[1,512]{1,0:T(1,128)S(1)}, s32[1,512]{1,0:T(1,128)}, u32[]{:S(2)}) copy-start(s32[1,512]{1,0:T(1,128)} %param.16) | copy-start | bytes 6148
  7.2 105.8 %all-gather.2.cloned.1.call-start = ((), (), s32[]{:S(2)}) async-start(), calls=%async_computation.1 | async-start | bytes 1114112 | tf_op jit(solution)/shard_map/all_gather | solution.py:81
  7.2 23.7 %collective-permute-start = (bf16[1,2,32,512]{3,2,1,0:T(8,128)(2,1)}, bf16[1,2,32,512]{3,2,1,0:T(8,128)(2,1)S(1)}, u32[]{:S(2)}, u32[]{:S(2)}) collective-permute-start(bf16[1,2,32,512]{3,2,1,0:T(8,128)(2,1)} %param.11), channel_id=1, source_target_pairs={{0,32},{32,64},{64,96},{96,128},{128,160},{160,192},{192,224},{224... | collective-permute-start | bytes 196616 | tf_op jit(solution)/shard_map/ppermute | solution.py:27
  11.3 29.9 %collective-permute-start.8 = (bf16[1,2,32,512]{3,2,1,0:T(8,128)(2,1)}, bf16[1,2,32,512]{3,2,1,0:T(8,128)(2,1)S(1)}, u32[]{:S(2)}, u32[]{:S(2)}) collective-permute-start(bf16[1,2,32,512]{3,2,1,0:T(8,128)(2,1)} %param.11), channel_id=1, source_target_pairs={{32,0},{64,32},{96,64},{128,96},{160,128},{192,160},{224,192},{256... | collective-permute-start | bytes 196616 | tf_op jit(solution)/shard_map/ppermute | solution.py:32
  29.8 20.1 %copy-start.20 = (s32[1,32]{1,0:T(1,128)S(1)}, s32[1,32]{1,0:T(1,128)}, u32[]{:S(2)}) copy-start(s32[1,32]{1,0:T(1,128)} %param.18) | copy-start | bytes 388
  29.8 28.8 %copy-start.21 = (s32[1,32]{1,0:T(1,128)S(1)}, s32[1,32]{1,0:T(1,128)}, u32[]{:S(2)}) copy-start(s32[1,32]{1,0:T(1,128)} %param.17) | copy-start | bytes 388
  29.8 29.4 %copy-start.1 = (bf16[8,1,48,512]{2,0,1,3:T(8,128)(2,1)S(1)}, bf16[8,1,48,512]{2,0,1,3:T(8,128)(2,1)}, u32[]{:S(2)}) copy-start(bf16[8,1,48,512]{2,0,1,3:T(8,128)(2,1)} %get-tuple-element.4) | copy-start | bytes 1179652
  30.9 29.7 %copy-start.9 = (bf16[1,2,32,512]{3,2,1,0:T(8,128)(2,1)}, bf16[1,2,32,512]{3,2,1,0:T(8,128)(2,1)S(1)}, u32[]{:S(2)}) copy-start(bf16[1,2,32,512]{3,2,1,0:T(8,128)(2,1)S(1)} %collective-permute-done) | copy-start | bytes 196612
  30.9 8.3 %collective-permute-start.1 = (bf16[1,2,32,512]{3,2,1,0:T(8,128)(2,1)S(1)}, bf16[1,2,32,512]{3,2,1,0:T(8,128)(2,1)S(1)}, u32[]{:S(2)}, u32[]{:S(2)}) collective-permute-start(bf16[1,2,32,512]{3,2,1,0:T(8,128)(2,1)S(1)} %collective-permute-done), channel_id=1, source_target_pairs={{0,32},{32,64},{64,96},{96,128},{128,160},{160,192},{192,224},{224... | collective-permute-start | bytes 196616 | tf_op jit(solution)/shard_map/ppermute | solution.py:27
  39.2 10.6 %copy-start.11 = (bf16[1,2,32,512]{3,2,1,0:T(8,128)(2,1)}, bf16[1,2,32,512]{3,2,1,0:T(8,128)(2,1)S(1)}, u32[]{:S(2)}) copy-start(bf16[1,2,32,512]{3,2,1,0:T(8,128)(2,1)S(1)} %collective-permute-done.1) | copy-start | bytes 196612
  39.2 8.6 %collective-permute-start.2 = (bf16[1,2,32,512]{3,2,1,0:T(8,128)(2,1)S(1)}, bf16[1,2,32,512]{3,2,1,0:T(8,128)(2,1)S(1)}, u32[]{:S(2)}, u32[]{:S(2)}) collective-permute-start(bf16[1,2,32,512]{3,2,1,0:T(8,128)(2,1)S(1)} %collective-permute-done.1), channel_id=1, source_target_pairs={{0,32},{32,64},{64,96},{96,128},{128,160},{160,192},{192,224},{224... | collective-permute-start | bytes 196616 | tf_op jit(solution)/shard_map/ppermute | solution.py:27
  41.2 19.4 %copy-start.7 = (bf16[1,2,32,512]{3,2,1,0:T(8,128)(2,1)}, bf16[1,2,32,512]{3,2,1,0:T(8,128)(2,1)S(1)}, u32[]{:S(2)}) copy-start(bf16[1,2,32,512]{3,2,1,0:T(8,128)(2,1)S(1)} %collective-permute-done.8) | copy-start | bytes 196612
  41.2 8.7 %collective-permute-start.9 = (bf16[1,2,32,512]{3,2,1,0:T(8,128)(2,1)S(1)}, bf16[1,2,32,512]{3,2,1,0:T(8,128)(2,1)}, u32[]{:S(2)}, u32[]{:S(2)}) collective-permute-start(bf16[1,2,32,512]{3,2,1,0:T(8,128)(2,1)S(1)} %collective-permute-done.8), channel_id=1, source_target_pairs={{32,0},{64,32},{96,64},{128,96},{160,128},{192,160},{224,192},{256... | collective-permute-start | bytes 196616 | tf_op jit(solution)/shard_map/ppermute | solution.py:32
  47.9 8.7 %copy-start.13 = (bf16[1,2,32,512]{3,2,1,0:T(8,128)(2,1)}, bf16[1,2,32,512]{3,2,1,0:T(8,128)(2,1)S(1)}, u32[]{:S(2)}) copy-start(bf16[1,2,32,512]{3,2,1,0:T(8,128)(2,1)S(1)} %collective-permute-done.2) | copy-start | bytes 196612
  47.9 8.7 %collective-permute-start.3 = (bf16[1,2,32,512]{3,2,1,0:T(8,128)(2,1)S(1)}, bf16[1,2,32,512]{3,2,1,0:T(8,128)(2,1)}, u32[]{:S(2)}, u32[]{:S(2)}) collective-permute-start(bf16[1,2,32,512]{3,2,1,0:T(8,128)(2,1)S(1)} %collective-permute-done.2), channel_id=1, source_target_pairs={{0,32},{32,64},{64,96},{96,128},{128,160},{160,192},{192,224},{224... | collective-permute-start | bytes 196616 | tf_op jit(solution)/shard_map/ppermute | solution.py:27
  49.9 13.4 %collective-permute-start.10 = (bf16[1,2,32,512]{3,2,1,0:T(8,128)(2,1)}, bf16[1,2,32,512]{3,2,1,0:T(8,128)(2,1)}, u32[]{:S(2)}, u32[]{:S(2)}) collective-permute-start(bf16[1,2,32,512]{3,2,1,0:T(8,128)(2,1)} %collective-permute-done.9), channel_id=1, source_target_pairs={{32,0},{64,32},{96,64},{128,96},{160,128},{192,160},{224,192},{256... | collective-permute-start | bytes 196616 | tf_op jit(solution)/shard_map/ppermute | solution.py:32
  56.6 13.4 %collective-permute-start.4 = (bf16[1,2,32,512]{3,2,1,0:T(8,128)(2,1)}, bf16[1,2,32,512]{3,2,1,0:T(8,128)(2,1)}, u32[]{:S(2)}, u32[]{:S(2)}) collective-permute-start(bf16[1,2,32,512]{3,2,1,0:T(8,128)(2,1)} %collective-permute-done.3), channel_id=1, source_target_pairs={{0,32},{32,64},{64,96},{96,128},{128,160},{160,192},{192,224},{224... | collective-permute-start | bytes 196616 | tf_op jit(solution)/shard_map/ppermute | solution.py:27
  61.4 10.6 %copy-start.16 = (s32[32]{0:T(128)S(1)}, s32[32]{0:T(128)}, u32[]{:S(2)}) copy-start(s32[32]{0:T(128)} %fusion.26) | copy-start | bytes 388
  61.4 39.6 %copy-start.14 = (bf16[1,2,32,512]{3,2,1,0:T(8,128)(2,1)S(1)}, bf16[1,2,32,512]{3,2,1,0:T(8,128)(2,1)}, u32[]{:S(2)}) copy-start(bf16[1,2,32,512]{3,2,1,0:T(8,128)(2,1)} %copy-done.13) | copy-start | bytes 196612
  61.4 40.2 %copy-start.12 = (bf16[1,2,32,512]{3,2,1,0:T(8,128)(2,1)S(1)}, bf16[1,2,32,512]{3,2,1,0:T(8,128)(2,1)}, u32[]{:S(2)}) copy-start(bf16[1,2,32,512]{3,2,1,0:T(8,128)(2,1)} %copy-done.11) | copy-start | bytes 196612
  61.4 40.8 %copy-start.10 = (bf16[1,2,32,512]{3,2,1,0:T(8,128)(2,1)S(1)}, bf16[1,2,32,512]{3,2,1,0:T(8,128)(2,1)}, u32[]{:S(2)}) copy-start(bf16[1,2,32,512]{3,2,1,0:T(8,128)(2,1)} %copy-done.9) | copy-start | bytes 196612
  61.4 41.5 %copy-start.6 = (bf16[1,2,32,512]{3,2,1,0:T(8,128)(2,1)S(1)}, bf16[1,2,32,512]{3,2,1,0:T(8,128)(2,1)}, u32[]{:S(2)}) copy-start(bf16[1,2,32,512]{3,2,1,0:T(8,128)(2,1)} %param.11) | copy-start | bytes 196612
  61.4 42.1 %copy-start.8 = (bf16[1,2,32,512]{3,2,1,0:T(8,128)(2,1)S(1)}, bf16[1,2,32,512]{3,2,1,0:T(8,128)(2,1)}, u32[]{:S(2)}) copy-start(bf16[1,2,32,512]{3,2,1,0:T(8,128)(2,1)} %copy-done.7) | copy-start | bytes 196612
  63.3 8.7 %collective-permute-start.11 = (bf16[1,2,32,512]{3,2,1,0:T(8,128)(2,1)}, bf16[1,2,32,512]{3,2,1,0:T(8,128)(2,1)S(1)}, u32[]{:S(2)}, u32[]{:S(2)}) collective-permute-start(bf16[1,2,32,512]{3,2,1,0:T(8,128)(2,1)} %collective-permute-done.10), channel_id=1, source_target_pairs={{32,0},{64,32},{96,64},{128,96},{160,128},{192,160},{224,192},{256... | collective-permute-start | bytes 196616 | tf_op jit(solution)/shard_map/ppermute | solution.py:32
  70.0 8.7 %collective-permute-start.5 = (bf16[1,2,32,512]{3,2,1,0:T(8,128)(2,1)}, bf16[1,2,32,512]{3,2,1,0:T(8,128)(2,1)S(1)}, u32[]{:S(2)}, u32[]{:S(2)}) collective-permute-start(bf16[1,2,32,512]{3,2,1,0:T(8,128)(2,1)} %collective-permute-done.4), channel_id=1, source_target_pairs={{0,32},{32,64},{64,96},{96,128},{128,160},{160,192},{192,224},{224... | collective-permute-start | bytes 196616 | tf_op jit(solution)/shard_map/ppermute | solution.py:27
  72.0 8.7 %collective-permute-start.12 = (bf16[1,2,32,512]{3,2,1,0:T(8,128)(2,1)S(1)}, bf16[1,2,32,512]{3,2,1,0:T(8,128)(2,1)S(1)}, u32[]{:S(2)}, u32[]{:S(2)}) collective-permute-start(bf16[1,2,32,512]{3,2,1,0:T(8,128)(2,1)S(1)} %collective-permute-done.11), channel_id=1, source_target_pairs={{32,0},{64,32},{96,64},{128,96},{160,128},{192,160},{224,192},{256... | collective-permute-start | bytes 196616 | tf_op jit(solution)/shard_map/ppermute | solution.py:32
  78.7 8.7 %collective-permute-start.6 = (bf16[1,2,32,512]{3,2,1,0:T(8,128)(2,1)S(1)}, bf16[1,2,32,512]{3,2,1,0:T(8,128)(2,1)S(1)}, u32[]{:S(2)}, u32[]{:S(2)}) collective-permute-start(bf16[1,2,32,512]{3,2,1,0:T(8,128)(2,1)S(1)} %collective-permute-done.5), channel_id=1, source_target_pairs={{0,32},{32,64},{64,96},{96,128},{128,160},{160,192},{192,224},{224... | collective-permute-start | bytes 196616 | tf_op jit(solution)/shard_map/ppermute | solution.py:27
  80.6 8.6 %collective-permute-start.13 = (bf16[1,2,32,512]{3,2,1,0:T(8,128)(2,1)S(1)}, bf16[1,2,32,512]{3,2,1,0:T(8,128)(2,1)S(1)}, u32[]{:S(2)}, u32[]{:S(2)}) collective-permute-start(bf16[1,2,32,512]{3,2,1,0:T(8,128)(2,1)S(1)} %collective-permute-done.12), channel_id=1, source_target_pairs={{32,0},{64,32},{96,64},{128,96},{160,128},{192,160},{224,192},{256... | collective-permute-start | bytes 196616 | tf_op jit(solution)/shard_map/ppermute | solution.py:32
  87.3 8.8 %collective-permute-start.7 = (bf16[1,2,32,512]{3,2,1,0:T(8,128)(2,1)S(1)}, bf16[1,2,32,512]{3,2,1,0:T(8,128)(2,1)S(1)}, u32[]{:S(2)}, u32[]{:S(2)}) collective-permute-start(bf16[1,2,32,512]{3,2,1,0:T(8,128)(2,1)S(1)} %collective-permute-done.6), channel_id=1, source_target_pairs={{0,32},{32,64},{64,96},{96,128},{128,160},{160,192},{192,224},{224... | collective-permute-start | bytes 196616 | tf_op jit(solution)/shard_map/ppermute | solution.py:27
  89.3 19.6 %collective-permute-start.14 = (bf16[1,2,32,512]{3,2,1,0:T(8,128)(2,1)S(1)}, bf16[1,2,32,512]{3,2,1,0:T(8,128)(2,1)S(1)}, u32[]{:S(2)}, u32[]{:S(2)}) collective-permute-start(bf16[1,2,32,512]{3,2,1,0:T(8,128)(2,1)S(1)} %collective-permute-done.13), channel_id=1, source_target_pairs={{32,0},{64,32},{96,64},{128,96},{160,128},{192,160},{224,192},{256... | collective-permute-start | bytes 196616 | tf_op jit(solution)/shard_map/ppermute | solution.py:32
  113.0 3.2 %copy-start = (bf16[1,2,512,512]{3,2,1,0:T(8,128)(2,1)S(1)}, bf16[1,2,512,512]{3,2,1,0:T(8,128)(2,1)}, u32[]{:S(2)}) copy-start(bf16[1,2,512,512]{3,2,1,0:T(8,128)(2,1)} %all-gather.2.cloned.1.call-done) | copy-start | bytes 3145732
  (6 other events, 13.1 us)
Sparse Core Ops, SparseCore 0:
  17.0 57.6 all-gather.1
